TPU v7x, 32 devices: a whole 2x2x4 slice. The times are simulated.
32 devices in a mesh: groups: 2 (over y), req: 4 (over z), head: 2 (over x), sub: 2 (over core).
Axes of the slice: x: 2, y: 2, z: 4, core: 2. Of those that a mesh axis runs over, the one named last changes fastest.
Arguments:
- hidden_in: bfloat16 [1024, 8192], P(('groups', 'req')), parts along dimension 0, may hold values from -3 to 3
- q_weight: bfloat16 [8192, 8192], P('req', ('head', 'sub')), may hold values from -0.0625 to 0.0625
- q_gain: float32 [128], replicated, may hold values from 0.1 to 1.9
- key_cache: bfloat16 [8, 1601, 1024], P(('groups', 'req'), None, 'head'), parts along dimension 0, may hold values from -64 to 64
- value_cache: bfloat16 [8, 1601, 1024], P(('groups', 'req'), None, 'head'), parts along dimension 0, may hold values from -8 to 8
- out_weight: bfloat16 [8192, 8192], P(('head', 'sub'), 'req'), may hold values from -0.09375 to 0.09375
- req_image: int32 [1024], P(('groups', 'req')), parts along dimension 0, may hold values from 0 to 3, as said below
- image_count: int32 [1024], P(('groups', 'req')), parts along dimension 0, may hold values from 0 to 1, as said below
- image_home: int32 [8], P('groups'), parts along dimension 0, may hold values from 0 to 3, as said below
Outputs:
- layer_out: bfloat16 [1024, 8192], P(('groups', 'req'), ('head', 'sub')), parts along dimension 0
There are 2 independent parts, one for each index of `groups`. A program takes and returns all parts, laid end to end along the dimension named above; an argument that names none is the same for every part. Nothing has to cross between parts.
Inputs may be any that keep to these rules, and one draw needn't show every extreme that they name: Requests with image_count 0 attend to nothing; in each aligned block of 128 requests at most a quarter have image_count 0. In each aligned block of 128 requests, at most 64 requests with image_count 1 have one and the same value of image_home[req_image]; in every block exactly 64 of them share one value, and that value is the same for all blocks. `image_home`: each cache row holds exactly one image.
All inputs are finite; a program needn't handle non-finite values.
Results may differ from a plain program's by a relative error of at most 0.025.
Values may be sent and summed in bfloat16 or wider, within the bound.
No kernel may reach another device: no remote copies, remote signals or barrier semaphores. Data moves between devices by JAX's collectives and lax.ppermute only.
A program may use at most 128 MiB of HBM per device.

v0:
```python
import jax
import jax.numpy as jnp
from jax import lax
from jax.sharding import PartitionSpec as P

HQ = 64
KVH = 8


def normalize_heads(queries, q_gain, head_dim):
    row_count = queries.shape[0]
    per_head = queries.astype(jnp.float32).reshape(row_count, -1, head_dim)
    inv_rms = lax.rsqrt(jnp.mean(per_head * per_head, axis=2, keepdims=True) + 1e-05)
    return (per_head * inv_rms * q_gain).reshape(row_count, -1).astype(jnp.bfloat16)


def exchange_sum(parts, axis, count, index):
    total = lax.dynamic_index_in_dim(parts, index, axis=0, keepdims=False).astype(jnp.float32)
    for shift in range(1, count):
        outgoing = lax.dynamic_index_in_dim(parts, (index + shift) % count, axis=0, keepdims=False)
        incoming = lax.ppermute(outgoing, axis, [(i, (i + shift) % count) for i in range(count)])
        total = total + incoming.astype(jnp.float32)
    return total.astype(jnp.bfloat16)


def local(
    hidden_in,
    q_weight,
    q_gain,
    key_cache,
    value_cache,
    out_weight,
    req_image,
    image_count,
    image_home,
):
    req_count = lax.axis_size("req")
    local_rows = hidden_in.shape[0]
    q_cols = q_weight.shape[1]
    head_dim = q_gain.shape[0]
    group_size = HQ // KVH
    heads_here = q_cols // head_dim
    sub_count = lax.axis_size("sub")
    sub_index = lax.axis_index("sub")
    block_width = hidden_in.shape[1] // req_count
    part_width = block_width // sub_count
    by_block = hidden_in.reshape(local_rows, req_count, sub_count, part_width)
    my_part = lax.dynamic_index_in_dim(by_block, sub_index, axis=2, keepdims=False)
    spread_part = lax.all_to_all(my_part, "req", split_axis=1, concat_axis=0, tiled=True)
    spread_part = spread_part.reshape(req_count * local_rows, part_width)
    spread_cols = jnp.zeros((req_count * local_rows, block_width), spread_part.dtype)
    spread_cols = lax.dynamic_update_slice_in_dim(
        spread_cols, spread_part, sub_index * part_width, 1
    )
    for shift in range(1, sub_count):
        other_part = lax.ppermute(
            spread_part, "sub", [(i, (i + shift) % sub_count) for i in range(sub_count)]
        )
        spread_cols = lax.dynamic_update_slice_in_dim(
            spread_cols, other_part, (sub_index - shift) % sub_count * part_width, 1
        )
    query_sum = lax.psum_scatter(
        jnp.dot(spread_cols, q_weight, preferred_element_type=jnp.float32).astype(jnp.bfloat16),
        "req",
        scatter_dimension=0,
        tiled=True,
    )
    queries = lax.optimization_barrier(query_sum)
    normalized = normalize_heads(queries, q_gain, head_dim)
    capacity = 2 * local_rows // req_count
    slot_total = req_count * capacity
    table_ids = lax.broadcasted_iota(jnp.int32, (local_rows, image_home.shape[0]), 1)
    home_rows = jnp.sum(jnp.where(req_image[:, None] == table_ids, image_home[None, :], 0), axis=1)
    wanted = image_count == 1
    dest_ids = lax.broadcasted_iota(jnp.int32, (local_rows, req_count), 1)
    to_dest = ((home_rows[:, None] == dest_ids) & wanted[:, None]).astype(jnp.int32)
    earlier = jnp.cumsum(to_dest, axis=0) - to_dest
    position = home_rows * capacity + jnp.sum(earlier * to_dest, axis=1)
    slot_ids = lax.broadcasted_iota(jnp.int32, (slot_total, local_rows), 0)
    dispatch = ((slot_ids == position[None, :]) & wanted[None, :]).astype(jnp.bfloat16)
    outgoing = jnp.dot(dispatch, normalized, preferred_element_type=jnp.float32).astype(
        jnp.bfloat16
    )
    outgoing = outgoing.reshape(req_count, capacity, q_cols)
    kv_count = max(1, heads_here // group_size)
    per_kv = heads_here // kv_count
    kv_first = sub_index * heads_here // group_size
    keys_here = lax.dynamic_slice_in_dim(
        key_cache[0], kv_first * head_dim, kv_count * head_dim, 1
    ).reshape(-1, kv_count, head_dim)
    values_here = lax.dynamic_slice_in_dim(
        value_cache[0], kv_first * head_dim, kv_count * head_dim, 1
    ).reshape(-1, kv_count, head_dim)
    score_scale = head_dim ** (-0.5)
    arrived = lax.all_to_all(outgoing, "req", split_axis=0, concat_axis=0, tiled=True)
    sources = arrived.shape[0]
    slot_count = arrived.shape[1]
    flat_rows = arrived.reshape(sources * slot_count, kv_count, per_kv, head_dim)
    scores = (
        jnp.einsum("mkgd,tkd->kgmt", flat_rows, keys_here, preferred_element_type=jnp.float32)
        * score_scale
    )
    row_peak = jnp.max(scores, axis=3, keepdims=True)
    weights = jnp.exp(scores - row_peak)
    probs = (weights / jnp.sum(weights, axis=3, keepdims=True)).astype(jnp.bfloat16)
    mixed_heads = jnp.einsum(
        "kgmt,tkd->mkgd", probs, values_here, preferred_element_type=jnp.float32
    )
    replies = mixed_heads.astype(jnp.bfloat16).reshape(sources, slot_count, q_cols)
    returned = lax.all_to_all(replies, "req", split_axis=0, concat_axis=0, tiled=True)
    attended = lax.dot_general(
        dispatch,
        returned.reshape(slot_total, q_cols),
        (((0,), (0,)), ((), ())),
        preferred_element_type=jnp.float32,
    ).astype(jnp.bfloat16)
    partial_cols = jnp.dot(
        lax.all_gather(attended, "req", axis=0, tiled=True),
        out_weight,
        preferred_element_type=jnp.float32,
    ).astype(jnp.bfloat16)
    hs_count = lax.axis_size("head") * sub_count
    hs_index = lax.axis_index("head") * sub_count + sub_index
    req_index = lax.axis_index("req")
    head_count = lax.axis_size("head")
    by_group = partial_cols.reshape(sub_count, -1, partial_cols.shape[1])
    owner_sums = exchange_sum(by_group, "sub", sub_count, sub_index)
    owner_sums = owner_sums.reshape(head_count, -1, partial_cols.shape[1])
    owner_sums = exchange_sum(owner_sums, "head", head_count, lax.axis_index("head"))
    per_hs = req_count // hs_count
    out_block = partial_cols.shape[1]
    owner_sums = owner_sums.reshape(per_hs, local_rows, out_block)
    arrived_blocks = []
    for step in range(per_hs):
        chunk = lax.dynamic_index_in_dim(
            owner_sums, (req_index + step) % per_hs, axis=0, keepdims=False
        )
        pairs = []
        for c in range(req_count):
            for h in range(head_count):
                for u in range(sub_count):
                    j = u * head_count + h
                    k = j * per_hs + (c + step) % per_hs
                    src = c * hs_count + h * sub_count + u
                    pairs.append((src, k * hs_count + c // per_hs))
        arrived_blocks.append(lax.ppermute(chunk, ("req", "head", "sub"), pairs))
    stacked = jnp.stack(arrived_blocks)
    order = (req_index % per_hs - jnp.arange(per_hs)) % per_hs
    head_total = jnp.take(stacked, order, axis=0)
    head_total = jnp.transpose(head_total, (1, 0, 2)).reshape(local_rows, per_hs * out_block)
    head_total = head_total.astype(jnp.float32)
    out_width = head_total.shape[1]
    residual = lax.dynamic_slice_in_dim(hidden_in, hs_index * out_width, out_width, 1)
    return (residual.astype(jnp.float32) + head_total).astype(jnp.bfloat16)


def solution(mesh):
    in_specs = (
        P(("groups", "req"), None),
        P("req", ("head", "sub")),
        P(),
        P(("groups", "req"), None, "head"),
        P(("groups", "req"), None, "head"),
        P(("head", "sub"), "req"),
        P(("groups", "req")),
        P(("groups", "req")),
        P("groups"),
    )
    out_specs = P(("groups", "req"), ("head", "sub"))
    return jax.shard_map(local, mesh=mesh, in_specs=in_specs, out_specs=out_specs, check_vma=False)
```

profile of v0, /device:TPU:1, one launch (start us, length us, event | category | flops | bytes accessed | tf_op | source)
XLA Modules:
  0.0 288.7 jit_solution(2909639808181706036)
XLA Ops:
  6.5 3.2 %copy.35 = bf16[128,8192]{0,1:T(8,128)(2,1)S(1)} copy(bf16[128,8192]{1,0:T(8,128)(2,1)} %param.9) | data formatting | bytes 4194304 | tf_op args[0]
  10.4 30.1 %all_to_all.25 = bf16[128,4,1024]{2,0,1:T(8,128)(2,1)S(1)} all-to-all(bf16[128,4,1024]{2,0,1:T(8,128)(2,1)S(1)} %bitcast.76), channel_id=1, replica_groups=mesh['groups'=2,'req'=4,'head'=2,'sub'=2] {'req'}, dimensions={1} | all-to-all | bytes 2097152 | tf_op jit(solution)/shard_map/all_to_all | solution.py:49
  40.5 1.8 collective-permute-start
  42.7 1.9 collective-permute-done
  44.7 9.1 %convolution_convert_fusion.1 = bf16[512,2048]{1,0:T(8,128)(2,1)} fusion(bf16[512,2048]{1,0:T(8,128)(2,1)S(1)} %constant_dynamic-update-slice_fusion, bf16[2048,2048]{1,0:T(8,128)(2,1)} %param.10), kind=kOutput, calls=%fused_computation.11 | convolution fusion | flops 4296015872 | bytes 12582912 | tf_op jit(solution)/shard_map/dot_general | solution.py:63
  55.2 41.4 %reduce-scatter.2.cloned.1.call-done = bf16[128,2048]{1,0:T(8,128)(2,1)} async-done(((bf16[512,2048]{1,0:T(8,128)(2,1)}), bf16[128,2048]{1,0:T(8,128)(2,1)}) %reduce-scatter.2.cloned.1.call-update) | async-done | bytes 524304 | tf_op jit(solution)/shard_map/reduce_scatter | solution.py:62
  98.8 1.6 convolution_convert_fusion.2
  100.4 3.5 %all-to-all-start.1 = ((bf16[4,64,2048]{2,1,0:T(8,128)(2,1)}), bf16[4,64,2048]{2,1,0:T(8,128)(2,1)S(1)}, u32[]{:S(2)}, u32[]{:S(2)}) async-start(bf16[4,64,2048]{2,1,0:T(8,128)(2,1)} %bitcast.12), calls=%async_computation.2 | async-start | bytes 2097152 | tf_op jit(solution)/shard_map/all_to_all | solution.py:95
  104.1 1.5 constant_dynamic-slice_fusion.1
  105.6 1.4 copy.34
  107.7 21.4 %all-to-all-done.1 = bf16[4,64,2048]{2,1,0:T(8,128)(2,1)S(1)} async-done(((bf16[4,64,2048]{2,1,0:T(8,128)(2,1)}), bf16[4,64,2048]{2,1,0:T(8,128)(2,1)S(1)}, u32[]{:S(2)}, u32[]{:S(2)}) %all-to-all-start.1) | async-done | bytes 1048608 | tf_op jit(solution)/shard_map/all_to_all | solution.py:95
  129.3 14.5 %fusion.36 = (f32[2,8,256]{2,1,0:T(8,128)S(1)}, f32[2,8,256,1601]{2,3,1,0:T(8,128)}) fusion(bf16[1601,2,128,1]{0,2,3,1:T(8,128)(2,1)} %bitcast.81, bf16[256,2,8,128]{3,2,1,0:T(8,128)(2,1)S(1)} %bitcast.79), kind=kOutput, calls=%fused_computation.54 | convolution fusion | flops 1698444800 | bytes 28115456 | tf_op jit(solution)/shard_map/sub | solution.py:104
  143.8 11.1 %fusion.12 = bf16[256,2,8,128]{0,3,2,1:T(8,128)(2,1)S(1)} fusion(bf16[1601,2,128,1]{0,2,3,1:T(8,128)(2,1)S(1)} %bitcast.80, f32[2,8,256,1601]{2,3,1,0:T(8,128)} %get-tuple-element.6, f32[2,8,256]{2,1,0:T(8,128)S(1)} %get-tuple-element.5), kind=kOutput, calls=%fused_computation.17 | convolution fusion | flops 1692409856 | bytes 28115456 | tf_op jit(solution)/shard_map/kgmt,tkd->mkgd/dot_general | solution.py:106
  156.5 27.3 %all_to_all.26 = bf16[4,64,2048]{2,1,0:T(8,128)(2,1)S(1)} all-to-all(bf16[4,64,2048]{2,1,0:T(8,128)(2,1)S(1)} %reshape.85), channel_id=1, replica_groups=mesh['groups'=2,'req'=4,'head'=2,'sub'=2] {'req'}, dimensions={0} | all-to-all | bytes 2097152 | tf_op jit(solution)/shard_map/all_to_all | solution.py:110
  183.8 1.1 convolution_convert_fusion.3
  185.0 46.3 %all-gather.2.cloned.1.call-done = bf16[512,2048]{1,0:T(8,128)(2,1)} async-done(((bf16[128,2048]{1,0:T(8,128)(2,1)}), bf16[512,2048]{1,0:T(8,128)(2,1)}) %all-gather.2.cloned.1.call-update) | async-done | bytes 2097168 | tf_op jit(solution)/shard_map/all_gather | solution.py:118
  231.3 8.5 %convolution_convert_fusion = bf16[512,2048]{1,0:T(8,128)(2,1)S(1)} fusion(bf16[512,2048]{1,0:T(8,128)(2,1)} %all-gather.2.cloned.1.call-done, bf16[2048,2048]{1,0:T(8,128)(2,1)} %param.14), kind=kOutput, calls=%fused_computation.10 | convolution fusion | flops 4296015872 | bytes 12582912 | tf_op jit(solution)/shard_map/dot_general | solution.py:117
  240.7 2.4 collective-permute-done.1
  243.1 1.6 fusion.10
  244.8 1.3 collective-permute-start.2
  246.0 11.9 %collective-permute-done.2 = bf16[128,2048]{1,0:T(8,128)(2,1)S(1)} collective-permute-done((bf16[128,2048]{1,0:T(8,128)(2,1)S(1)}, bf16[128,2048]{1,0:T(8,128)(2,1)S(1)}, u32[]{:S(2)}, u32[]{:S(2)}) %collective-permute-start.2) | collective-permute-done | bytes 524320 | tf_op jit(solution)/shard_map/ppermute | solution.py:21
  258.1 3.8 %collective-permute-start.3 = (bf16[128,2048]{1,0:T(8,128)(2,1)S(1)}, bf16[128,2048]{1,0:T(8,128)(2,1)S(1)}, u32[]{:S(2)}, u32[]{:S(2)}) collective-permute-start(bf16[128,2048]{1,0:T(8,128)(2,1)S(1)} %fusion.16), channel_id=1, source_target_pairs={{0,0},{1,8},{2,4},{3,12},{4,1},{5,9},{6,5},{7,13},{8,2},{9,10},{10... | collective-permute-start | bytes 1572872 | tf_op jit(solution)/shard_map/ppermute | solution.py:146
  261.9 18.0 %collective-permute-done.3 = bf16[128,2048]{1,0:T(8,128)(2,1)S(1)} collective-permute-done((bf16[128,2048]{1,0:T(8,128)(2,1)S(1)}, bf16[128,2048]{1,0:T(8,128)(2,1)S(1)}, u32[]{:S(2)}, u32[]{:S(2)}) %collective-permute-start.3) | collective-permute-done | bytes 524320 | tf_op jit(solution)/shard_map/ppermute | solution.py:146
  279.8 2.0 add_convert_fusion
  (43 shorter events, 8.3 us)
Async XLA Ops:
  6.5 48.6 %copy-start = (f32[128]{0:T(128)S(1)}, f32[128]{0:T(128)}, u32[]{:S(2)}) copy-start(f32[128]{0:T(128)} %param.11) | copy-start | bytes 1540
  6.5 90.0 %reduce-scatter.2.cloned.1.call-start = ((), (), s32[]{:S(2)}) async-start(), calls=%async_computation.4 | async-start | bytes 2621440 | tf_op jit(solution)/shard_map/reduce_scatter | solution.py:62
  40.5 4.1 %collective-permute-start = (bf16[512,1024]{1,0:T(8,128)(2,1)S(1)}, bf16[512,1024]{1,0:T(8,128)(2,1)S(1)}, u32[]{:S(2)}, u32[]{:S(2)}) collective-permute-start(bf16[512,1024]{1,0:T(8,128)(2,1)S(1)} %bitcast.69), channel_id=1, source_target_pairs={{0,1},{1,0},{2,3},{3,2},{4,5},{5,4},{6,7},{7,6},{8,9},{9,8},{10,11... | collective-permute-start | bytes 3145736 | tf_op jit(solution)/shard_map/ppermute | solution.py:56
  53.8 0.7 copy-start.3
  53.8 0.7 copy-start.4
  53.8 0.8 copy-start.5
  97.7 1.1 copy-start.2
  100.4 28.7 %all-to-all-start.1 = ((bf16[4,64,2048]{2,1,0:T(8,128)(2,1)}), bf16[4,64,2048]{2,1,0:T(8,128)(2,1)S(1)}, u32[]{:S(2)}, u32[]{:S(2)}) async-start(bf16[4,64,2048]{2,1,0:T(8,128)(2,1)} %bitcast.12), calls=%async_computation.2 | async-start | bytes 2097152 | tf_op jit(solution)/shard_map/all_to_all | solution.py:95
  103.9 127.4 %all-gather.2.cloned.1.call-start = ((), (), s32[]{:S(2)}) async-start(), calls=%async_computation.5 | async-start | bytes 2621440 | tf_op jit(solution)/shard_map/all_gather | solution.py:118
  239.9 3.2 %collective-permute-start.1 = (bf16[256,2048]{1,0:T(8,128)(2,1)S(1)}, bf16[256,2048]{1,0:T(8,128)(2,1)}, u32[]{:S(2)}, u32[]{:S(2)}) collective-permute-start(bf16[256,2048]{1,0:T(8,128)(2,1)S(1)} %dynamic-slice_bitcast_fusion), channel_id=1, source_target_pairs={{0,1},{1,0},{2,3},{3,2},{4,5},{5,4},{6,7},{7,6},{8,9},{9,8},{10,11... | collective-permute-start | bytes 3145736 | tf_op jit(solution)/shard_map/ppermute | solution.py:21
  244.7 37.2 %copy-start.1 = (f32[128]{0:T(128)S(1)}, f32[128]{0:T(128)}, u32[]{:S(2)}) copy-start(f32[128]{0:T(128)} %param.11) | copy-start | bytes 1540
  244.8 13.2 %collective-permute-start.2 = (bf16[128,2048]{1,0:T(8,128)(2,1)S(1)}, bf16[128,2048]{1,0:T(8,128)(2,1)S(1)}, u32[]{:S(2)}, u32[]{:S(2)}) collective-permute-start(bf16[128,2048]{1,0:T(8,128)(2,1)S(1)} %dynamic-slice_bitcast_fusion.1), channel_id=1, source_target_pairs={{0,2},{2,0},{1,3},{3,1},{4,6},{6,4},{5,7},{7,5},{8,10},{10,8},{9,1... | collective-permute-start | bytes 1572872 | tf_op jit(solution)/shard_map/ppermute | solution.py:21
  258.1 21.7 %collective-permute-start.3 = (bf16[128,2048]{1,0:T(8,128)(2,1)S(1)}, bf16[128,2048]{1,0:T(8,128)(2,1)S(1)}, u32[]{:S(2)}, u32[]{:S(2)}) collective-permute-start(bf16[128,2048]{1,0:T(8,128)(2,1)S(1)} %fusion.16), channel_id=1, source_target_pairs={{0,0},{1,8},{2,4},{3,12},{4,1},{5,9},{6,5},{7,13},{8,2},{9,10},{10... | collective-permute-start | bytes 1572872 | tf_op jit(solution)/shard_map/ppermute | solution.py:146
Sparse Core Ops, SparseCore 0:
  54.0 42.5 reduce-scatter.1
  185.1 46.1 all-gather.1
where the time goes:
time: 289 us
  waiting for transfers between devices  143 us (49%)
  blocking collectives  57.4 us (20%)
  matrix products  46 us (16%)
  between operations  13.7 us (5%)
  starting transfers between devices  11.3 us (4%)
  local copies, waits for them, and re-layouts  11.2 us (4%)
  other arithmetic  5.88 us (2%)
    all_gather x1, waiting for transfers between devices, local(): lax.all_gather(attended, 'req', axis=0, tiled=True)  46.3 us
    reduce_scatter x1, waiting for transfers between devices, local(): lax.psum_scatter(jnp.dot(spread_cols, q_weight, preferred_element_type=jn...  41.4 us
    all_to_all x1, blocking collectives, local(): lax.all_to_all(my_part, 'req', split_axis=1, concat_axis=0, tiled=True)  30.1 us
    all_to_all x1, blocking collectives, local(): lax.all_to_all(replies, 'req', split_axis=0, concat_axis=0, tiled=True)  27.3 us
    all_to_all x1, waiting for transfers between devices, local(): lax.all_to_all(outgoing, 'req', split_axis=0, concat_axis=0, tiled=True)  21.4 us
    ppermute x1, waiting for transfers between devices, local(): arrived_blocks.append(lax.ppermute(chunk, ('req', 'head', 'sub'), pairs))  18 us
    sub x1, matrix products, local(): weights = jnp.exp(scores - row_peak)  14.5 us
    ppermute x2, waiting for transfers between devices, exchange_sum(): lax.ppermute(outgoing, axis, [(i, (i + shift) % count) for i in range(cou...  14.4 us
  transfers between devices with their start and end apart: 7, of which 7 were waited for; matrix products, arithmetic and copies ran while one was open for 2% of the time, Pallas kernels for 0%

commit v1 on v0

--- a/solution.py
+++ b/solution.py
@@ -5,6 +5,29 @@
 
 HQ = 64
 KVH = 8
+
+
+def divide_region_for(peer_axis, obj):
+    y1, piece_now, x_now = (lax.axis_size(peer_axis), lax.axis_index(peer_axis), obj.shape[0])
+    lanes = tuple(((nth, (nth + 1) % y1) for nth in range(y1)))
+    stack_in = tuple(((nth, (nth - 1) % y1) for nth in range(y1)))
+    mixed_arr = jnp.zeros((*obj.shape[:0], y1 * x_now, *obj.shape[1:]), obj.dtype)
+    mixed_arr = lax.dynamic_update_slice_in_dim(mixed_arr, obj, piece_now * x_now, axis=0)
+    known = w_next = obj
+    back = y1 // 2
+    no = 1
+    while no < back + 1:
+        known = lax.ppermute(known, peer_axis, perm=lanes)
+        mixed_arr = lax.dynamic_update_slice_in_dim(
+            mixed_arr, known, (piece_now - no) % y1 * x_now, axis=0
+        )
+        if no < y1 - back:
+            w_next = lax.ppermute(w_next, peer_axis, stack_in)
+            mixed_arr = lax.dynamic_update_slice_in_dim(
+                mixed_arr, w_next, (piece_now + no) % y1 * x_now, axis=0
+            )
+        no = no + 1
+    return mixed_arr
 
 
 def normalize_heads(queries, q_gain, head_dim):
@@ -115,9 +138,7 @@
         preferred_element_type=jnp.float32,
     ).astype(jnp.bfloat16)
     partial_cols = jnp.dot(
-        lax.all_gather(attended, "req", axis=0, tiled=True),
-        out_weight,
-        preferred_element_type=jnp.float32,
+        divide_region_for("req", attended), out_weight, preferred_element_type=jnp.float32
     ).astype(jnp.bfloat16)
     hs_count = lax.axis_size("head") * sub_count
     hs_index = lax.axis_index("head") * sub_count + sub_index

time: 289 us -> 286 us (0.990)
  blocking collectives: 57.4 us -> 30.1 us
  waiting for transfers between devices: 143 us -> 155 us
  starting transfers between devices: 11.3 us -> 17.9 us
  local copies, waits for them, and re-layouts: 11.2 us -> 16 us
    all_gather x1 -> x0, waiting for transfers between devices: 46.3 us -> none  [local(): lax.all_gather(attended, 'req', axis=0, tiled=True)]
    ppermute x0 -> x3, waiting for transfers between devices: none -> 31.4 us  [the longest x2 22.8 us: divide_region_for(): known = lax.ppermute(known, peer_axis, perm=lanes)]
    all_to_all x1 -> x0, blocking collectives: 27.3 us -> none  [local(): lax.all_to_all(replies, 'req', split_axis=0, concat_axis=0, tiled=True)]
    all_to_all x0 -> x1, waiting for transfers between devices: none -> 25.2 us  [local(): lax.all_to_all(replies, 'req', split_axis=0, concat_axis=0, tiled=True)]
    all_to_all x0 -> x1, starting transfers between devices: none -> 3.51 us  [local(): lax.all_to_all(replies, 'req', split_axis=0, concat_axis=0, tiled=True)]
    ppermute x0 -> x3, starting transfers between devices: none -> 3.27 us  [the longest x1 3.26 us: divide_region_for(): w_next = lax.ppermute(w_next, peer_axis, stack_in)]
  transfers between devices with their start and end apart: 7 -> 10, of which waited for: 7 -> 10; matrix products, arithmetic and copies ran while one was open for 2% -> 2% of each run, Pallas kernels for 0% -> 0%
where the time goes in v1:
time: 286 us; the launch traced here: 285 us
  waiting for transfers between devices  155 us (54%)
  matrix products  46 us (16%)
  blocking collectives  30.1 us (11%)
  starting transfers between devices  17.9 us (6%)
  local copies, waits for them, and re-layouts  16 us (6%)
  between operations  13.7 us (5%)
  other arithmetic  5.88 us (2%)
    reduce_scatter x1, waiting for transfers between devices, local(): lax.psum_scatter(jnp.dot(spread_cols, q_weight, preferred_element_type=jn...  41.4 us
    all_to_all x1, blocking collectives, local(): lax.all_to_all(my_part, 'req', split_axis=1, concat_axis=0, tiled=True)  30.1 us
    all_to_all x1, waiting for transfers between devices, local(): lax.all_to_all(replies, 'req', split_axis=0, concat_axis=0, tiled=True)  25.2 us
    ppermute x2, waiting for transfers between devices, divide_region_for(): known = lax.ppermute(known, peer_axis, perm=lanes)  22.8 us
    all_to_all x1, waiting for transfers between devices, local(): lax.all_to_all(outgoing, 'req', split_axis=0, concat_axis=0, tiled=True)  21.5 us
    ppermute x1, waiting for transfers between devices, local(): arrived_blocks.append(lax.ppermute(chunk, ('req', 'head', 'sub'), pairs))  19.8 us
    sub x1, matrix products, local(): weights = jnp.exp(scores - row_peak)  14.6 us
    ppermute x2, waiting for transfers between devices, exchange_sum(): lax.ppermute(outgoing, axis, [(i, (i + shift) % count) for i in range(cou...  14.4 us
  transfers between devices with their start and end apart: 10, of which 10 were waited for; matrix products, arithmetic and copies ran while one was open for 2% of the time, Pallas kernels for 0%

profile of v1, /device:TPU:1, one launch (start us, length us, event | category | flops | bytes accessed | tf_op | source)
XLA Modules:
  0.0 285.0 jit_solution(14634861111898528705)
XLA Ops:
  6.5 3.2 %copy.35 = bf16[128,8192]{0,1:T(8,128)(2,1)S(1)} copy(bf16[128,8192]{1,0:T(8,128)(2,1)} %param.9) | data formatting | bytes 4194304 | tf_op args[0]
  10.4 30.1 %all_to_all.25 = bf16[128,4,1024]{2,0,1:T(8,128)(2,1)S(1)} all-to-all(bf16[128,4,1024]{2,0,1:T(8,128)(2,1)S(1)} %bitcast.76), channel_id=1, replica_groups=mesh['groups'=2,'req'=4,'head'=2,'sub'=2] {'req'}, dimensions={1} | all-to-all | bytes 2097152 | tf_op jit(solution)/shard_map/all_to_all | solution.py:72
  40.5 1.8 collective-permute-start
  42.7 1.9 collective-permute-done
  44.7 9.1 %convolution_convert_fusion.1 = bf16[512,2048]{1,0:T(8,128)(2,1)} fusion(bf16[512,2048]{1,0:T(8,128)(2,1)S(1)} %constant_dynamic-update-slice_fusion.4, bf16[2048,2048]{1,0:T(8,128)(2,1)} %param.10), kind=kOutput, calls=%fused_computation.11 | convolution fusion | flops 4296015872 | bytes 12582912 | tf_op jit(solution)/shard_map/dot_general | solution.py:86
  55.2 41.4 %reduce-scatter.2.cloned.1.call-done = bf16[128,2048]{1,0:T(8,128)(2,1)} async-done(((bf16[512,2048]{1,0:T(8,128)(2,1)}), bf16[128,2048]{1,0:T(8,128)(2,1)}) %reduce-scatter.2.cloned.1.call-update) | async-done | bytes 524304 | tf_op jit(solution)/shard_map/reduce_scatter | solution.py:85
  100.3 3.7 %all-to-all-start.1 = ((bf16[4,64,2048]{2,1,0:T(8,128)(2,1)}), bf16[4,64,2048]{2,1,0:T(8,128)(2,1)S(1)}, u32[]{:S(2)}, u32[]{:S(2)}) async-start(bf16[4,64,2048]{2,1,0:T(8,128)(2,1)} %bitcast.12), calls=%async_computation.2 | async-start | bytes 2097152 | tf_op jit(solution)/shard_map/all_to_all | solution.py:118
  107.6 21.5 %all-to-all-done.1 = bf16[4,64,2048]{2,1,0:T(8,128)(2,1)S(1)} async-done(((bf16[4,64,2048]{2,1,0:T(8,128)(2,1)}), bf16[4,64,2048]{2,1,0:T(8,128)(2,1)S(1)}, u32[]{:S(2)}, u32[]{:S(2)}) %all-to-all-start.1) | async-done | bytes 1048608 | tf_op jit(solution)/shard_map/all_to_all | solution.py:118
  129.3 14.6 %fusion.36 = (f32[2,8,256]{2,1,0:T(8,128)S(1)}, f32[2,8,256,1601]{2,3,1,0:T(8,128)}) fusion(bf16[1601,2,128,1]{0,2,3,1:T(8,128)(2,1)} %bitcast.81, bf16[256,2,8,128]{3,2,1,0:T(8,128)(2,1)S(1)} %bitcast.79), kind=kOutput, calls=%fused_computation.58 | convolution fusion | flops 1698444800 | bytes 28115456 | tf_op jit(solution)/shard_map/sub | solution.py:127
  143.8 11.1 %fusion.12 = bf16[256,2,8,128]{0,3,2,1:T(8,128)(2,1)S(1)} fusion(bf16[1601,2,128,1]{0,2,3,1:T(8,128)(2,1)S(1)} %bitcast.80, f32[2,8,256,1601]{2,3,1,0:T(8,128)} %get-tuple-element.6, f32[2,8,256]{2,1,0:T(8,128)S(1)} %get-tuple-element.5), kind=kOutput, calls=%fused_computation.17 | convolution fusion | flops 1692409856 | bytes 28115456 | tf_op jit(solution)/shard_map/kgmt,tkd->mkgd/dot_general | solution.py:129
  157.3 3.5 %all-to-all-start.2 = ((bf16[4,64,2048]{2,1,0:T(8,128)(2,1)}), bf16[4,64,2048]{2,1,0:T(8,128)(2,1)S(1)}, u32[]{:S(2)}, u32[]{:S(2)}) async-start(bf16[4,64,2048]{2,1,0:T(8,128)(2,1)} %reshape.85), calls=%async_computation.3 | async-start | bytes 2097152 | tf_op jit(solution)/shard_map/all_to_all | solution.py:133
  160.8 25.2 %all-to-all-done.2 = bf16[4,64,2048]{2,1,0:T(8,128)(2,1)S(1)} async-done(((bf16[4,64,2048]{2,1,0:T(8,128)(2,1)}), bf16[4,64,2048]{2,1,0:T(8,128)(2,1)S(1)}, u32[]{:S(2)}, u32[]{:S(2)}) %all-to-all-start.2) | async-done | bytes 1048608 | tf_op jit(solution)/shard_map/all_to_all | solution.py:133
  188.8 3.3 %collective-permute-start.2 = (bf16[128,2048]{1,0:T(8,128)(2,1)S(1)}, bf16[128,2048]{1,0:T(8,128)(2,1)S(1)}, u32[]{:S(2)}, u32[]{:S(2)}) collective-permute-start(bf16[128,2048]{1,0:T(8,128)(2,1)S(1)} %get-tuple-element.8), channel_id=1, source_target_pairs={{0,12},{4,0},{8,4},{12,8},{1,13},{5,1},{9,5},{13,9},{2,14},{6,2},{... | collective-permute-start | bytes 1572872 | tf_op jit(solution)/shard_map/ppermute | solution.py:25
  192.0 10.6 %collective-permute-done.1 = bf16[128,2048]{1,0:T(8,128)(2,1)S(1)} collective-permute-done((bf16[128,2048]{1,0:T(8,128)(2,1)S(1)}, bf16[128,2048]{1,0:T(8,128)(2,1)S(1)}, u32[]{:S(2)}, u32[]{:S(2)}) %collective-permute-start.1) | collective-permute-done | bytes 524320 | tf_op jit(solution)/shard_map/ppermute | solution.py:20
  203.4 8.5 %collective-permute-done.2 = bf16[128,2048]{1,0:T(8,128)(2,1)S(1)} collective-permute-done((bf16[128,2048]{1,0:T(8,128)(2,1)S(1)}, bf16[128,2048]{1,0:T(8,128)(2,1)S(1)}, u32[]{:S(2)}, u32[]{:S(2)}) %collective-permute-start.2) | collective-permute-done | bytes 524320 | tf_op jit(solution)/shard_map/ppermute | solution.py:25
  212.8 12.3 %collective-permute-done.3 = bf16[128,2048]{1,0:T(8,128)(2,1)S(1)} collective-permute-done((bf16[128,2048]{1,0:T(8,128)(2,1)S(1)}, bf16[128,2048]{1,0:T(8,128)(2,1)S(1)}, u32[]{:S(2)}, u32[]{:S(2)}) %collective-permute-start.3) | collective-permute-done | bytes 524320 | tf_op jit(solution)/shard_map/ppermute | solution.py:20
  225.9 8.5 %convolution_convert_fusion = bf16[512,2048]{1,0:T(8,128)(2,1)S(1)} fusion(bf16[512,2048]{1,0:T(8,128)(2,1)} %constant_dynamic-update-slice_fusion, bf16[2048,2048]{1,0:T(8,128)(2,1)} %param.14), kind=kOutput, calls=%fused_computation.10 | convolution fusion | flops 4296015872 | bytes 12582912 | tf_op jit(solution)/shard_map/dot_general | solution.py:140
  234.5 2.4 collective-permute-start.4
  236.9 2.4 collective-permute-done.4
  239.4 1.6 fusion.10
  242.3 12.0 %collective-permute-done.5 = bf16[128,2048]{1,0:T(8,128)(2,1)S(1)} collective-permute-done((bf16[128,2048]{1,0:T(8,128)(2,1)S(1)}, bf16[128,2048]{1,0:T(8,128)(2,1)S(1)}, u32[]{:S(2)}, u32[]{:S(2)}) %collective-permute-start.5) | collective-permute-done | bytes 524320 | tf_op jit(solution)/shard_map/ppermute | solution.py:44
  254.4 1.9 collective-permute-start.6
  256.3 19.8 %collective-permute-done.6 = bf16[128,2048]{1,0:T(8,128)(2,1)S(1)} collective-permute-done((bf16[128,2048]{1,0:T(8,128)(2,1)S(1)}, bf16[128,2048]{1,0:T(8,128)(2,1)S(1)}, u32[]{:S(2)}, u32[]{:S(2)}) %collective-permute-start.6) | collective-permute-done | bytes 524320 | tf_op jit(solution)/shard_map/ppermute | solution.py:167
  276.1 2.0 add_convert_fusion
  (51 shorter events, 19.0 us)
Async XLA Ops:
  6.5 48.6 %copy-start = (f32[128]{0:T(128)S(1)}, f32[128]{0:T(128)}, u32[]{:S(2)}) copy-start(f32[128]{0:T(128)} %param.11) | copy-start | bytes 1540
  6.5 90.0 %reduce-scatter.2.cloned.1.call-start = ((), (), s32[]{:S(2)}) async-start(), calls=%async_computation.4 | async-start | bytes 2621440 | tf_op jit(solution)/shard_map/reduce_scatter | solution.py:85
  40.5 4.1 %collective-permute-start = (bf16[512,1024]{1,0:T(8,128)(2,1)S(1)}, bf16[512,1024]{1,0:T(8,128)(2,1)S(1)}, u32[]{:S(2)}, u32[]{:S(2)}) collective-permute-start(bf16[512,1024]{1,0:T(8,128)(2,1)S(1)} %bitcast.69), channel_id=1, source_target_pairs={{0,1},{1,0},{2,3},{3,2},{4,5},{5,4},{6,7},{7,6},{8,9},{9,8},{10,11... | collective-permute-start | bytes 3145736 | tf_op jit(solution)/shard_map/ppermute | solution.py:79
  53.8 0.7 copy-start.3
  53.8 0.7 copy-start.4
  53.8 0.8 copy-start.5
  97.7 1.1 copy-start.2
  100.3 28.7 %all-to-all-start.1 = ((bf16[4,64,2048]{2,1,0:T(8,128)(2,1)}), bf16[4,64,2048]{2,1,0:T(8,128)(2,1)S(1)}, u32[]{:S(2)}, u32[]{:S(2)}) async-start(bf16[4,64,2048]{2,1,0:T(8,128)(2,1)} %bitcast.12), calls=%async_computation.2 | async-start | bytes 2097152 | tf_op jit(solution)/shard_map/all_to_all | solution.py:118
  157.3 28.7 %all-to-all-start.2 = ((bf16[4,64,2048]{2,1,0:T(8,128)(2,1)}), bf16[4,64,2048]{2,1,0:T(8,128)(2,1)S(1)}, u32[]{:S(2)}, u32[]{:S(2)}) async-start(bf16[4,64,2048]{2,1,0:T(8,128)(2,1)} %reshape.85), calls=%async_computation.3 | async-start | bytes 2097152 | tf_op jit(solution)/shard_map/all_to_all | solution.py:133
  188.8 13.8 %collective-permute-start.1 = (bf16[128,2048]{1,0:T(8,128)(2,1)S(1)}, bf16[128,2048]{1,0:T(8,128)(2,1)S(1)}, u32[]{:S(2)}, u32[]{:S(2)}) collective-permute-start(bf16[128,2048]{1,0:T(8,128)(2,1)S(1)} %get-tuple-element.8), channel_id=1, source_target_pairs={{0,4},{4,8},{8,12},{12,0},{1,5},{5,9},{9,13},{13,1},{2,6},{6,10},{... | collective-permute-start | bytes 1572872 | tf_op jit(solution)/shard_map/ppermute | solution.py:20
  188.8 23.2 %collective-permute-start.2 = (bf16[128,2048]{1,0:T(8,128)(2,1)S(1)}, bf16[128,2048]{1,0:T(8,128)(2,1)S(1)}, u32[]{:S(2)}, u32[]{:S(2)}) collective-permute-start(bf16[128,2048]{1,0:T(8,128)(2,1)S(1)} %get-tuple-element.8), channel_id=1, source_target_pairs={{0,12},{4,0},{8,4},{12,8},{1,13},{5,1},{9,5},{13,9},{2,14},{6,2},{... | collective-permute-start | bytes 1572872 | tf_op jit(solution)/shard_map/ppermute | solution.py:25
  202.6 22.5 %collective-permute-start.3 = (bf16[128,2048]{1,0:T(8,128)(2,1)S(1)}, bf16[128,2048]{1,0:T(8,128)(2,1)S(1)}, u32[]{:S(2)}, u32[]{:S(2)}) collective-permute-start(bf16[128,2048]{1,0:T(8,128)(2,1)S(1)} %collective-permute-done.1), channel_id=1, source_target_pairs={{0,4},{4,8},{8,12},{12,0},{1,5},{5,9},{9,13},{13,1},{2,6},{6,10},{... | collective-permute-start | bytes 1572872 | tf_op jit(solution)/shard_map/ppermute | solution.py:20
  234.5 4.8 %collective-permute-start.4 = (bf16[256,2048]{1,0:T(8,128)(2,1)S(1)}, bf16[256,2048]{1,0:T(8,128)(2,1)}, u32[]{:S(2)}, u32[]{:S(2)}) collective-permute-start(bf16[256,2048]{1,0:T(8,128)(2,1)S(1)} %dynamic-slice_bitcast_fusion), channel_id=1, source_target_pairs={{0,1},{1,0},{2,3},{3,2},{4,5},{5,4},{6,7},{7,6},{8,9},{9,8},{10,11... | collective-permute-start | bytes 3145736 | tf_op jit(solution)/shard_map/ppermute | solution.py:44
  241.0 37.2 %copy-start.1 = (f32[128]{0:T(128)S(1)}, f32[128]{0:T(128)}, u32[]{:S(2)}) copy-start(f32[128]{0:T(128)} %param.11) | copy-start | bytes 1540
  241.0 13.2 %collective-permute-start.5 = (bf16[128,2048]{1,0:T(8,128)(2,1)S(1)}, bf16[128,2048]{1,0:T(8,128)(2,1)S(1)}, u32[]{:S(2)}, u32[]{:S(2)}) collective-permute-start(bf16[128,2048]{1,0:T(8,128)(2,1)S(1)} %dynamic-slice_bitcast_fusion.1), channel_id=1, source_target_pairs={{0,2},{2,0},{1,3},{3,1},{4,6},{6,4},{5,7},{7,5},{8,10},{10,8},{9,1... | collective-permute-start | bytes 1572872 | tf_op jit(solution)/shard_map/ppermute | solution.py:44
  254.4 21.7 %collective-permute-start.6 = (bf16[128,2048]{1,0:T(8,128)(2,1)S(1)}, bf16[128,2048]{1,0:T(8,128)(2,1)S(1)}, u32[]{:S(2)}, u32[]{:S(2)}) collective-permute-start(bf16[128,2048]{1,0:T(8,128)(2,1)S(1)} %fusion.16), channel_id=1, source_target_pairs={{0,0},{1,8},{2,4},{3,12},{4,1},{5,9},{6,5},{7,13},{8,2},{9,10},{10... | collective-permute-start | bytes 1572872 | tf_op jit(solution)/shard_map/ppermute | solution.py:167
Sparse Core Ops, SparseCore 0:
  54.0 42.5 reduce-scatter.1
